TPU v7x, 128 devices: a whole 4x4x4 slice. The times are simulated.
128 devices in a mesh: leaf: 16 (over y, z), ctx: 8 (over x, core).
Axes of the slice: x: 4, y: 4, z: 4, core: 2. Of those that a mesh axis runs over, the one named last changes fastest.
Arguments:
- query_key_value_rows: bfloat16 [16384, 7168], P(('leaf', 'ctx')), may hold values from -6 to 6
- cotangent: bfloat16 [16384, 5120], P(('leaf', 'ctx')), may hold values from -6 to 6
- out_weight: bfloat16 [5120, 5120], P('ctx'), may hold values from -0.078125 to 0.078125
- parents: int32 [16, 8], P('leaf'), may hold values from 0 to 6, as said below
- rollout_spans: int32 [16384], P('leaf'), may hold values from 64 to 4096
Outputs:
- qkv_grad: bfloat16 [16384, 7168], P(('leaf', 'ctx'))
- weight_grad: bfloat16 [5120, 5120], P('ctx')
Inputs may be any that keep to these rules, and one draw needn't show every extreme that they name: parents[t, 0] = 0, every later block's parent is an earlier block of the same tree, and the last block's parent is the block just before it.
All inputs are finite; a program needn't handle non-finite values.
Results may differ from a plain program's by a relative error of at most 0.012.
The roundings to bfloat16 on the way count: a program that leaves them out, or rounds other values in their place, can miss the bound.
Values may be sent and summed in bfloat16 or wider, within the bound.
No kernel may reach another device: no remote copies, remote signals or barrier semaphores. Data moves between devices by JAX's collectives and lax.ppermute only.
A program may use at most 192 MiB of HBM per device.

v0:
```python
import math
import jax
import jax.numpy as jnp
from jax import lax
from jax.sharding import PartitionSpec as P

QUERY_HEADS = 40
KEY_VALUE_HEADS = 8
HEAD_SIZE = 128
BLK = 128
log_base = 1024.0


def ancestors(parents):
    number = parents.shape[0]
    indices = jnp.arange(number, dtype=jnp.int32)

    def advance(iteration, state):
        current, reached = state
        current = jnp.sum(
            jnp.where(current[:, None] == indices[None, :], parents[None, :], 0), axis=1
        )
        return (current, reached | (current[:, None] == indices[None, :]))

    return lax.fori_loop(0, number, advance, (indices, indices[:, None] == indices[None, :]))[1]


def token_mask(reached, first_row, query_count, key_count):
    query_pos = first_row + jnp.arange(query_count, dtype=jnp.int32)
    key_pos = jnp.arange(key_count, dtype=jnp.int32)
    block_part = reached[first_row // BLK : (first_row + query_count) // BLK, : key_count // BLK]
    expanded = jnp.repeat(jnp.repeat(block_part, BLK, axis=0), BLK, axis=1)
    same_block = (query_pos // BLK)[:, None] == (key_pos // BLK)[None, :]
    return expanded & (jnp.logical_not(same_block) | (key_pos[None, :] <= query_pos[:, None]))


def span_softness(rollout_spans):
    return jnp.log(rollout_spans.astype(jnp.float32)) * (
        1.0 / (math.log(log_base) * math.sqrt(HEAD_SIZE))
    )


def contract_rows(left, right):
    return lax.dot_general(
        left, right, (((0,), (0,)), ((), ())), preferred_element_type=jnp.float32
    )


def contract_cols(left, right):
    return lax.dot_general(
        left, right, (((1,), (1,)), ((), ())), preferred_element_type=jnp.float32
    )


def local(query_key_value_rows, cotangent, out_weight, parents, rollout_spans):
    queries_per_group = QUERY_HEADS // KEY_VALUE_HEADS
    head_rows = lax.all_to_all(query_key_value_rows, "ctx", split_axis=1, concat_axis=0, tiled=True)
    tree_len = head_rows.shape[0]
    kv_local = head_rows.shape[1] // ((queries_per_group + 2) * HEAD_SIZE)
    heads_local = kv_local * queries_per_group
    grouped = head_rows.reshape(tree_len, kv_local, queries_per_group + 2, HEAD_SIZE)
    asking_matrix = grouped[:, :, :queries_per_group]
    lookup_matrix = grouped[:, :, queries_per_group]
    value_rows = grouped[:, :, queries_per_group + 1]
    softness_multiplier = span_softness(rollout_spans)
    reached = ancestors(parents[0])
    block_len = min(512, tree_len)
    block_total = tree_len // block_len
    masks = []
    total_parts = []
    attended_parts = []
    for block_id in range(block_total):
        opening_slot = block_id * block_len
        closing_slot = opening_slot + block_len
        allowed = token_mask(reached, opening_slot, block_len, closing_slot)
        masks.append(allowed)
        attention_logits = jnp.einsum(
            "zpyr,kpr->pyzk",
            asking_matrix[opening_slot:closing_slot],
            lookup_matrix[:closing_slot],
            preferred_element_type=jnp.float32,
        )
        attention_logits = jnp.where(
            allowed[None, None],
            attention_logits * softness_multiplier[opening_slot:closing_slot][None, None, :, None],
            -jnp.inf,
        )
        peak_score = jnp.max(attention_logits, axis=-1, keepdims=True)
        log_total = peak_score + jnp.log(
            jnp.sum(jnp.exp(attention_logits - peak_score), axis=-1, keepdims=True)
        )
        weights_low = jnp.exp(attention_logits - log_total).astype(jnp.bfloat16)
        attended_parts.append(
            jnp.einsum(
                "gjts,sgd->tgjd",
                weights_low,
                value_rows[:closing_slot],
                preferred_element_type=jnp.float32,
            ).astype(jnp.bfloat16)
        )
        total_parts.append(log_total[..., 0])
    attended = jnp.concatenate(attended_parts, axis=0)
    log_totals = jnp.concatenate(total_parts, axis=2)
    flat_out = attended.reshape(tree_len, heads_local * HEAD_SIZE)
    shard_rows = lax.all_gather(cotangent, "ctx", axis=0, tiled=True)
    weight_acc = contract_rows(flat_out, shard_rows)
    local_grad = contract_cols(shard_rows, out_weight).astype(jnp.bfloat16)
    weight_acc, output_gradient = (weight_acc, local_grad)
    weight_total = lax.psum(weight_acc, "leaf").astype(jnp.bfloat16)
    key_acc = jnp.zeros((tree_len, kv_local, HEAD_SIZE), jnp.float32)
    value_acc = jnp.zeros((tree_len, kv_local, HEAD_SIZE), jnp.float32)
    query_parts = []
    for head_id in range(heads_local):
        kv_id = head_id // queries_per_group
        inner = head_id % queries_per_group
        query_blocks = []
        for block_id in range(block_total):
            opening_slot = block_id * block_len
            closing_slot = opening_slot + block_len
            query_now = asking_matrix[opening_slot:closing_slot, kv_id, inner]
            keys_now = lookup_matrix[:closing_slot, kv_id]
            values_now = value_rows[:closing_slot, kv_id]
            line_multiplier = softness_multiplier[opening_slot:closing_slot][:, None]
            attention_logits = jnp.where(
                masks[block_id], contract_cols(query_now, keys_now) * line_multiplier, -jnp.inf
            )
            attention_probabilities = jnp.exp(
                attention_logits - log_totals[kv_id, inner, opening_slot:closing_slot][:, None]
            )
            grad_rows = output_gradient[
                opening_slot:closing_slot, head_id * HEAD_SIZE : (head_id + 1) * HEAD_SIZE
            ]
            own_rows = attended[opening_slot:closing_slot, kv_id, inner]
            probability_cotangent = contract_cols(grad_rows, values_now)
            middle_point = jnp.sum(
                grad_rows.astype(jnp.float32) * own_rows.astype(jnp.float32), axis=1
            )
            logit_cotangent = (
                attention_probabilities
                * (probability_cotangent - middle_point[:, None])
                * line_multiplier
            ).astype(jnp.bfloat16)
            query_blocks.append(
                jnp.dot(logit_cotangent, keys_now, preferred_element_type=jnp.float32).astype(
                    jnp.bfloat16
                )
            )
            key_acc = key_acc.at[:closing_slot, kv_id].add(
                contract_rows(logit_cotangent, query_now)
            )
            value_acc = value_acc.at[:closing_slot, kv_id].add(
                contract_rows(attention_probabilities.astype(jnp.bfloat16), grad_rows)
            )
        query_parts.append(jnp.concatenate(query_blocks, axis=0))
    query_grad = jnp.stack(query_parts, axis=1).reshape(
        tree_len, kv_local, queries_per_group, HEAD_SIZE
    )
    gradients = jnp.concatenate(
        [
            query_grad,
            key_acc.astype(jnp.bfloat16)[:, :, None],
            value_acc.astype(jnp.bfloat16)[:, :, None],
        ],
        axis=2,
    )
    gradients = gradients.reshape(tree_len, kv_local * (queries_per_group + 2) * HEAD_SIZE)
    returned = lax.all_to_all(gradients, "ctx", split_axis=0, concat_axis=1, tiled=True)
    return (returned, weight_total)


def solution(mesh):
    placed = (
        P(("leaf", "ctx"), None),
        P(("leaf", "ctx"), None),
        P("ctx", None),
        P("leaf", None),
        P("leaf"),
    )
    return jax.shard_map(
        local,
        mesh=mesh,
        in_specs=placed,
        out_specs=(P(("leaf", "ctx"), None), P("ctx", None)),
        check_vma=False,
    )
```

profile of v0, /device:TPU:0, one launch (start us, length us, event | category | flops | bytes accessed | tf_op | source)
XLA Modules:
  0.0 449.4 jit_solution(9614831033946304401)
XLA Ops:
  7.2 0.7 all-gather.2.cloned.1.call-update
  7.9 3.9 copy.35
  11.8 4.5 %all-to-all-start = ((bf16[128,8,896]{0,2,1:T(8,128)(2,1)}), bf16[128,8,896]{0,2,1:T(8,128)(2,1)S(1)}, u32[]{:S(2)}, u32[]{:S(2)}) async-start(bf16[128,8,896]{0,2,1:T(8,128)(2,1)} %bitcast.482), calls=%async_computation | async-start | bytes 3670016 | tf_op jit(solution)/shard_map/all_to_all | solution.py:57
  16.3 2.2 while.34
  18.6 1.6 broadcast_in_dim.71
  21.0 1.6 broadcast_in_dim.76
  22.6 0.8 fusion.14
  23.5 1.0 copy.42
  24.5 30.3 %all-to-all-done = bf16[128,8,896]{0,2,1:T(8,128)(2,1)S(1)} async-done(((bf16[128,8,896]{0,2,1:T(8,128)(2,1)}), bf16[128,8,896]{0,2,1:T(8,128)(2,1)S(1)}, u32[]{:S(2)}, u32[]{:S(2)}) %all-to-all-start) | async-done | bytes 1835040 | tf_op jit(solution)/shard_map/all_to_all | solution.py:57
  54.8 2.4 copy.36
  57.2 3.0 reshape.966
  60.3 1.0 fusion.8
  61.3 1.1 exponential_reduce_fusion.1
  62.4 1.8 fusion.3
  64.3 2.2 exponential_reduce_fusion
  66.5 1.6 fusion.54
  68.1 3.6 fusion.51
  71.7 1.3 pad_maximum_fusion.1
  73.0 1.4 fusion.37
  74.4 1.4 fusion.33
  75.9 1.5 fusion.35
  77.3 1.4 fusion.31
  78.7 2.4 fusion.39
  81.1 2.0 subtract_exponential_fusion.1
  83.1 2.1 subtract_exponential_fusion.3
  85.2 2.1 subtract_exponential_fusion.2
  87.3 2.0 subtract_exponential_fusion.4
  89.3 2.0 subtract_exponential_fusion
  91.3 11.9 %convolution_convert_fusion = bf16[1024,640]{0,1:T(8,128)(2,1)S(1)} fusion(bf16[1024,5120]{1,0:T(8,128)(2,1)} %all-gather.2.cloned.1.call-done, bf16[640,5120]{1,0:T(8,128)(2,1)} %param.49), kind=kOutput, calls=%fused_computation.35 | convolution fusion | flops 6711541760 | bytes 18350080 | tf_op jit(solution)/shard_map/dot_general | solution.py:50
  103.6 1.1 copy-done.4
  104.8 0.5 multiply_convert_fusion.4
  110.8 14.2 %fusion.218 = f32[640,5120]{1,0:T(8,128)} fusion(bf16[1024,640]{0,1:T(8,128)(2,1)S(1)} %bitcast.489, bf16[1024,5120]{1,0:T(8,128)(2,1)} %all-gather.2.cloned.1.call-done), kind=kOutput, calls=%fused_computation.328 | convolution fusion | flops 6710886400 | bytes 24903680 | tf_op jit(solution)/shard_map/dot_general | solution.py:44
  125.0 0.5 multiply_convert_fusion.1
  126.0 0.6 copy-done.3
  126.6 0.5 multiply_convert_fusion.3
  127.5 0.6 copy-done.2
  128.2 0.5 multiply_convert_fusion.2
  130.0 0.5 fusion.62
  130.9 0.5 fusion.63
  136.0 0.7 copy-done
  136.7 0.5 fusion.71
  137.2 0.5 multiply_convert_fusion
  139.1 2.5 copy.45
  141.6 2.0 copy.56
  143.7 1.5 copy.46
  145.2 3.6 all-to-all-start.1
  148.8 290.7 %all-reduce.2 = bf16[640,5120]{1,0:T(8,128)(2,1)} all-reduce(f32[640,5120]{1,0:T(8,128)} %fusion.218), channel_id=1, replica_groups=mesh['leaf'=16,'ctx'=8] {'leaf'}, use_global_device_ids=true, to_apply=%region_17.18 | all-reduce | flops 3276800 | bytes 19660800 | tf_op jit(solution)/shard_map/psum | solution.py:109
  439.5 2.9 copy.47
  (115 shorter events, 17.4 us)
Async XLA Ops:
  7.2 84.1 %all-gather.2.cloned.1.call-start = ((), (), s32[]{:S(2)}) async-start(), calls=%async_computation.2 | async-start | bytes 11796480 | tf_op jit(solution)/shard_map/all_gather | solution.py:105
  11.8 4.5 %copy-start.16 = (s32[1,8]{1,0:T(1,128)S(1)}, s32[1,8]{1,0:T(1,128)}, u32[]{:S(2)}) copy-start(s32[1,8]{1,0:T(1,128)} %param.50) | copy-start | bytes 100
  11.8 43.0 %all-to-all-start = ((bf16[128,8,896]{0,2,1:T(8,128)(2,1)}), bf16[128,8,896]{0,2,1:T(8,128)(2,1)S(1)}, u32[]{:S(2)}, u32[]{:S(2)}) async-start(bf16[128,8,896]{0,2,1:T(8,128)(2,1)} %bitcast.482), calls=%async_computation | async-start | bytes 3670016 | tf_op jit(solution)/shard_map/all_to_all | solution.py:57
  20.2 4.3 copy-start.15
  20.5 55.3 %copy-start.14 = (pred[512,512]{1,0:T(32,128)(4,1)}, pred[512,512]{1,0:T(32,128)(4,1)S(1)}, u32[]{:S(2)}) copy-start(pred[512,512]{1,0:T(32,128)(4,1)S(1)} %fusion.92) | copy-start | bytes 786436
  68.1 3.6 copy-start.11
  71.7 2.7 copy-start.9
  91.3 11.9 %copy-start.12 = (bf16[512,1,5,128]{0,3,2,1:T(8,128)(2,1)S(1)}, bf16[512,1,5,128]{0,3,2,1:T(8,128)(2,1)}, u32[]{:S(2)}) copy-start(bf16[512,1,5,128]{0,3,2,1:T(8,128)(2,1)} %copy-done.11) | copy-start | bytes 1966084
  91.3 12.1 %copy-start.10 = (bf16[512,1,5,128]{0,3,2,1:T(8,128)(2,1)S(1)}, bf16[512,1,5,128]{0,3,2,1:T(8,128)(2,1)}, u32[]{:S(2)}) copy-start(bf16[512,1,5,128]{0,3,2,1:T(8,128)(2,1)} %copy-done.9) | copy-start | bytes 1966084
  103.2 1.6 copy-start.4
  105.3 1.2 copy-start.5
  105.7 1.4 copy-start.8
  106.8 1.3 copy-start.7
  108.7 1.2 copy-start.6
  109.4 1.4 copy-start.13
  110.8 14.2 %copy-start.1 = (f32[512,1024]{1,0:T(8,128)S(1)}, f32[512,1024]{1,0:T(8,128)}, u32[]{:S(2)}) copy-start(f32[512,1024]{1,0:T(8,128)} %subtract_exponential_fusion.1) | copy-start | bytes 6291460
  125.0 1.6 copy-start.3
  126.6 1.6 copy-start.2
  135.1 1.6 copy-start
  145.2 294.3 %all-to-all-start.1 = ((bf16[8,128,896]{1,2,0:T(8,128)(2,1)}), bf16[8,128,896]{1,2,0:T(8,128)(2,1)S(1)}, u32[]{:S(2)}, u32[]{:S(2)}) async-start(bf16[8,128,896]{1,2,0:T(8,128)(2,1)} %copy.46), calls=%async_computation.1 | async-start | bytes 3670016 | tf_op jit(solution)/shard_map/all_to_all | solution.py:167
Sparse Core Ops, SparseCore 0:
  9.7 74.7 all-gather.1
where the time goes:
time: 454 us; the launch traced here: 449 us
  blocking collectives  291 us (64%)
  matrix products  68.7 us (15%)
  waiting for transfers between devices  31 us (7%)
  local copies, waits for them, and re-layouts  27.2 us (6%)
  between operations  14.9 us (3%)
  other arithmetic  8.79 us (2%)
  starting transfers between devices  8.15 us (2%)
    psum x1, blocking collectives, local(): weight_total = lax.psum(weight_acc, 'leaf').astype(jnp.bfloat16)  291 us
    dot_general x21, matrix products, contract_cols(): lax.dot_general(left, right, (((1,), (1,)), ((), ())), preferred_element_...  34.3 us
    all_to_all x1, waiting for transfers between devices, local(): lax.all_to_all(query_key_value_rows, 'ctx', split_axis=1, concat_axis=0,...  30.3 us
    dot_general x21, matrix products, contract_rows(): lax.dot_general(left, right, (((0,), (0,)), ((), ())), preferred_element_...  22.7 us
    unnamed x38, local copies, waits for them, and re-layouts  13 us
  transfers between devices with their start and end apart: 3, of which 1 were waited for; matrix products, arithmetic and copies ran while one was open for 11% of the time, Pallas kernels for 0%

commit v1 on v0

--- a/solution.py
+++ b/solution.py
@@ -9,6 +9,29 @@
 HEAD_SIZE = 128
 BLK = 128
 log_base = 1024.0
+
+
+def cut_along(value, dim, count):
+    shape = value.shape
+    blocks = value.reshape(*shape[:dim], count, shape[dim] // count, *shape[dim + 1 :])
+    return jnp.moveaxis(blocks, dim, 0)
+
+
+def joined_along(tiles, dim):
+    lengths = list(tiles.shape[1:])
+    lengths[dim] *= tiles.shape[0]
+    return jnp.moveaxis(tiles, 0, dim).reshape(lengths)
+
+
+def swapped_with_each(array, axis, split_dim, concat_dim):
+    size, mine = (lax.axis_size(axis), lax.axis_index(axis))
+    blocks = cut_along(array, split_dim, size)
+    outs = [blocks[mine]]
+    for step in range(1, size):
+        sent = blocks[mine ^ step]
+        outs.append(lax.ppermute(sent, axis, [(i, i ^ step) for i in range(size)]))
+    blocks = jnp.stack(outs)[mine ^ jnp.arange(size)]
+    return joined_along(blocks, concat_dim)
 
 
 def ancestors(parents):
@@ -54,7 +77,7 @@
 
 def local(query_key_value_rows, cotangent, out_weight, parents, rollout_spans):
     queries_per_group = QUERY_HEADS // KEY_VALUE_HEADS
-    head_rows = lax.all_to_all(query_key_value_rows, "ctx", split_axis=1, concat_axis=0, tiled=True)
+    head_rows = swapped_with_each(query_key_value_rows, "ctx", 1, 0)
     tree_len = head_rows.shape[0]
     kv_local = head_rows.shape[1] // ((queries_per_group + 2) * HEAD_SIZE)
     heads_local = kv_local * queries_per_group

time: 454 us -> 499 us (1.099)
  local copies, waits for them, and re-layouts: 27.2 us -> 68.6 us
  waiting for transfers between devices: 31 us -> 23.7 us
  matrix products: 68.7 us -> 73.8 us
    all_to_all x1 -> x0, waiting for transfers between devices: 30.3 us -> none  [local(): lax.all_to_all(query_key_value_rows, 'ctx', split_axis=1, concat_axis=0,...]
    unnamed x38 -> x105, local copies, waits for them, and re-layouts: 13 us -> 40.5 us
    ppermute x0 -> x7, waiting for transfers between devices: none -> 23 us  [swapped_with_each(): outs.append(lax.ppermute(sent, axis, [(i, i ^ step) for i in range(size)]))]
    dot_general x2, matrix products: 5.18 us -> 16.5 us  [local(): jnp.einsum('gjts,sgd->tgjd', weights_low, value_rows[:closing_slot], pref...]
    another operation x0 -> x11, local copies, waits for them, and re-layouts: none -> 10.4 us
    ppermute x0 -> x7, starting transfers between devices: none -> 8.23 us  [swapped_with_each(): outs.append(lax.ppermute(sent, axis, [(i, i ^ step) for i in range(size)]))]
    slice x0 -> x3, local copies, waits for them, and re-layouts: none -> 5.75 us  [the longest x1 3.69 us: local(): values_now = value_rows[:closing_slot, kv_id]]
  transfers between devices with their start and end apart: 3 -> 9, of which waited for: 1 -> 4; matrix products, arithmetic and copies ran while one was open for 11% -> 20% of each run, Pallas kernels for 0% -> 0%
where the time goes in v1:
time: 499 us; the launch traced here: 492 us
  blocking collectives  290 us (58%)
  matrix products  73.8 us (15%)
  local copies, waits for them, and re-layouts  68.6 us (14%)
  waiting for transfers between devices  23.7 us (5%)
  between operations  15.4 us (3%)
  starting transfers between devices  11.9 us (2%)
  other arithmetic  8.72 us (2%)
    psum x1, blocking collectives, local(): weight_total = lax.psum(weight_acc, 'leaf').astype(jnp.bfloat16)  290 us
    unnamed x105, local copies, waits for them, and re-layouts  40.5 us
    dot_general x21, matrix products, contract_cols(): lax.dot_general(left, right, (((1,), (1,)), ((), ())), preferred_element_...  31.8 us
    ppermute x7, waiting for transfers between devices, swapped_with_each(): outs.append(lax.ppermute(sent, axis, [(i, i ^ step) for i in range(size)]))  23 us
    dot_general x21, matrix products, contract_rows(): lax.dot_general(left, right, (((0,), (0,)), ((), ())), preferred_element_...  18.5 us
    dot_general x2, matrix products, local(): jnp.einsum('gjts,sgd->tgjd', weights_low, value_rows[:closing_slot], pref...  16.5 us
  transfers between devices with their start and end apart: 9, of which 4 were waited for; matrix products, arithmetic and copies ran while one was open for 20% of the time, Pallas kernels for 0%

profile of v1, /device:TPU:0, one launch (start us, length us, event | category | flops | bytes accessed | tf_op | source)
XLA Modules:
  0.0 492.4 jit_solution(16354595102000033225)
XLA Ops:
  7.9 3.3 copy.44
  13.8 1.6 collective-permute-start.1
  17.4 3.1 collective-permute-start.3
  21.4 2.2 while.34
  23.9 1.6 broadcast_in_dim.71
  25.9 1.6 broadcast_in_dim.76
  29.4 1.6 copy.59
  32.2 2.9 collective-permute-start.5
  38.4 3.7 collective-permute-done.3
  43.1 7.3 %collective-permute-done.4 = bf16[128,896]{1,0:T(8,128)(2,1)} collective-permute-done((bf16[128,896]{1,0:T(8,128)(2,1)}, bf16[128,896]{1,0:T(8,128)(2,1)}, u32[]{:S(2)}, u32[]{:S(2)}) %collective-permute-start.4) | collective-permute-done | bytes 229408 | tf_op jit(solution)/shard_map/ppermute | solution.py:32
  51.4 2.5 collective-permute-done.5
  53.9 9.5 %collective-permute-done.6 = bf16[128,896]{1,0:T(8,128)(2,1)S(1)} collective-permute-done((bf16[128,896]{1,0:T(8,128)(2,1)S(1)}, bf16[128,896]{1,0:T(8,128)(2,1)S(1)}, u32[]{:S(2)}, u32[]{:S(2)}) %collective-permute-start.6) | collective-permute-done | bytes 229408 | tf_op jit(solution)/shard_map/ppermute | solution.py:32
  63.5 2.0 gather_fusion
  65.4 3.9 reshape.1042
  69.4 1.9 fusion.203
  73.6 3.7 fusion.202
  77.3 1.7 copy.75
  80.0 1.7 copy.85
  81.8 1.7 copy.84
  83.5 1.7 copy.83
  85.2 1.7 copy.82
  87.0 1.7 copy.81
  88.7 1.7 copy.80
  90.5 1.7 copy.76
  92.2 1.8 copy.72
  93.9 1.7 copy.87
  95.7 1.8 copy.86
  100.5 2.3 fusion.3
  102.8 2.2 exponential_reduce_fusion
  105.0 1.6 fusion.54
  106.7 14.9 %fusion.51 = bf16[512,1,5,128]{0,3,2,1:T(8,128)(2,1)S(1)} fusion(f32[1024,512,5]{1,0,2:T(8,128)S(1)} %get-tuple-element.356, f32[5,512]{1,0:T(8,128)S(1)} %log_add_fusion, f32[512]{0:T(512)S(1)} %get-tuple-element.354, pred[512,1024]{0,1:T(8,128)(4,1)S(1)} %copy-done.11, bf16[1024,1,1,128]{0,3,2,1:T(8,128)(2,1)S(1)} %copy.79), kind=kOutput, calls=%fused_computation.80 | convolution fusion | flops 681902080 | bytes 11939840 | tf_op jit(solution)/shard_map/gjts,sgd->tgjd/dot_general | solution.py:117
  122.9 1.4 fusion.37
  124.3 1.4 fusion.35
  125.7 1.4 fusion.33
  127.2 1.4 fusion.31
  128.6 1.4 fusion.39
  130.0 2.0 subtract_exponential_fusion.1
  132.0 2.0 subtract_exponential_fusion.2
  134.1 2.1 subtract_exponential_fusion.3
  136.1 2.0 subtract_exponential_fusion.4
  138.9 11.8 %convolution_convert_fusion = bf16[1024,640]{0,1:T(8,128)(2,1)S(1)} fusion(bf16[1024,5120]{1,0:T(8,128)(2,1)} %all-gather.2.cloned.1.call-done, bf16[640,5120]{1,0:T(8,128)(2,1)} %param.49), kind=kOutput, calls=%fused_computation.36 | convolution fusion | flops 6711541760 | bytes 18350080 | tf_op jit(solution)/shard_map/dot_general | solution.py:73
  158.4 10.1 %fusion.208 = f32[640,5120]{1,0:T(8,128)} fusion(bf16[1024,640]{0,1:T(8,128)(2,1)S(1)} %bitcast.492, bf16[1024,5120]{1,0:T(8,128)(2,1)S(1)} %copy-done.38), kind=kOutput, calls=%fused_computation.327 | convolution fusion | flops 6710886400 | bytes 24903680 | tf_op jit(solution)/shard_map/dot_general | solution.py:67
  182.4 2.5 copy.62
  185.0 2.0 copy.90
  187.0 1.5 copy.63
  188.5 3.6 all-to-all-start
  192.1 290.1 %all-reduce.2 = bf16[640,5120]{1,0:T(8,128)(2,1)} all-reduce(f32[640,5120]{1,0:T(8,128)} %fusion.208), channel_id=1, replica_groups=mesh['leaf'=16,'ctx'=8] {'leaf'}, use_global_device_ids=true, to_apply=%region_17.18 | all-reduce | flops 3276800 | bytes 19660800 | tf_op jit(solution)/shard_map/psum | solution.py:132
  482.3 2.9 copy.64
  (209 shorter events, 46.8 us)
Async XLA Ops:
  7.2 131.7 %all-gather.2.cloned.1.call-start = ((), (), s32[]{:S(2)}) async-start(), calls=%async_computation.1 | async-start | bytes 11796480 | tf_op jit(solution)/shard_map/all_gather | solution.py:128
  11.3 10.1 %copy-start.39 = (s32[1,8]{1,0:T(1,128)S(1)}, s32[1,8]{1,0:T(1,128)}, u32[]{:S(2)}) copy-start(s32[1,8]{1,0:T(1,128)} %param.50) | copy-start | bytes 100
  12.1 11.7 %copy-start.37 = (s32[1024]{0:T(1024)S(1)}, s32[1024]{0:T(1024)}, u32[]{:S(2)}) copy-start(s32[1024]{0:T(1024)} %param.51) | copy-start | bytes 12292
  13.0 19.3 %collective-permute-start = (bf16[128,896]{1,0:T(8,128)(2,1)}, bf16[128,896]{1,0:T(8,128)(2,1)}, u32[]{:S(2)}, u32[]{:S(2)}) collective-permute-start(bf16[128,896]{1,0:T(8,128)(2,1)} %bitcast.3), channel_id=1, source_target_pairs={{0,1},{1,0},{2,3},{3,2},{4,5},{5,4},{6,7},{7,6},{8,9},{9,8},{10,11... | collective-permute-start | bytes 688136 | tf_op jit(solution)/shard_map/ppermute | solution.py:32
  13.8 22.3 %collective-permute-start.1 = (bf16[128,896]{1,0:T(8,128)(2,1)}, bf16[128,896]{1,0:T(8,128)(2,1)}, u32[]{:S(2)}, u32[]{:S(2)}) collective-permute-start(bf16[128,896]{1,0:T(8,128)(2,1)} %bitcast.5), channel_id=1, source_target_pairs={{0,2},{1,3},{2,0},{3,1},{4,6},{5,7},{6,4},{7,5},{8,10},{9,11},{10,... | collective-permute-start | bytes 688136 | tf_op jit(solution)/shard_map/ppermute | solution.py:32
  16.2 21.2 %collective-permute-start.2 = (bf16[128,896]{1,0:T(8,128)(2,1)}, bf16[128,896]{1,0:T(8,128)(2,1)}, u32[]{:S(2)}, u32[]{:S(2)}) collective-permute-start(bf16[128,896]{1,0:T(8,128)(2,1)} %bitcast.7), channel_id=1, source_target_pairs={{0,3},{1,2},{2,1},{3,0},{4,7},{5,6},{6,5},{7,4},{8,11},{9,10},{10,... | collective-permute-start | bytes 688136 | tf_op jit(solution)/shard_map/ppermute | solution.py:32
  17.4 24.8 %collective-permute-start.3 = (bf16[128,896]{1,0:T(8,128)(2,1)}, bf16[128,896]{1,0:T(8,128)(2,1)}, u32[]{:S(2)}, u32[]{:S(2)}) collective-permute-start(bf16[128,896]{1,0:T(8,128)(2,1)} %bitcast.9), channel_id=1, source_target_pairs={{0,4},{1,5},{2,6},{3,7},{4,0},{5,1},{6,2},{7,3},{8,12},{9,13},{10,... | collective-permute-start | bytes 688136 | tf_op jit(solution)/shard_map/ppermute | solution.py:32
  21.3 29.1 %collective-permute-start.4 = (bf16[128,896]{1,0:T(8,128)(2,1)}, bf16[128,896]{1,0:T(8,128)(2,1)}, u32[]{:S(2)}, u32[]{:S(2)}) collective-permute-start(bf16[128,896]{1,0:T(8,128)(2,1)} %bitcast.11), channel_id=1, source_target_pairs={{0,5},{1,4},{2,7},{3,6},{4,1},{5,0},{6,3},{7,2},{8,13},{9,12},{10,... | collective-permute-start | bytes 688136 | tf_op jit(solution)/shard_map/ppermute | solution.py:32
  32.2 21.6 %collective-permute-start.5 = (bf16[128,896]{1,0:T(8,128)(2,1)S(1)}, bf16[128,896]{1,0:T(8,128)(2,1)S(1)}, u32[]{:S(2)}, u32[]{:S(2)}) collective-permute-start(bf16[128,896]{1,0:T(8,128)(2,1)S(1)} %bitcast.497), channel_id=1, source_target_pairs={{0,6},{1,7},{2,4},{3,5},{4,2},{5,3},{6,0},{7,1},{8,14},{9,15},{10,... | collective-permute-start | bytes 688136 | tf_op jit(solution)/shard_map/ppermute | solution.py:32
  36.1 27.3 %collective-permute-start.6 = (bf16[128,896]{1,0:T(8,128)(2,1)S(1)}, bf16[128,896]{1,0:T(8,128)(2,1)S(1)}, u32[]{:S(2)}, u32[]{:S(2)}) collective-permute-start(bf16[128,896]{1,0:T(8,128)(2,1)S(1)} %bitcast.496), channel_id=1, source_target_pairs={{0,7},{1,6},{2,5},{3,4},{4,3},{5,2},{6,1},{7,0},{8,15},{9,14},{10,... | collective-permute-start | bytes 688136 | tf_op jit(solution)/shard_map/ppermute | solution.py:32
  97.4 0.9 copy-start.16
  99.4 1.1 copy-start.11
  102.8 2.2 copy-start.9
  106.7 14.9 %copy-start.14 = (bf16[512,1,5,128]{0,3,2,1:T(8,128)(2,1)}, bf16[512,1,5,128]{0,3,2,1:T(8,128)(2,1)S(1)}, u32[]{:S(2)}) copy-start(bf16[512,1,5,128]{0,3,2,1:T(8,128)(2,1)S(1)} %fusion.54) | copy-start | bytes 1966084
  121.6 2.7 copy-start.12
  121.6 1.3 copy-start.20
  121.6 2.7 copy-start.26
  122.8 2.9 copy-start.29
  122.9 4.3 copy-start.31
  124.3 4.3 copy-start.24
  125.7 4.3 copy-start.18
  128.6 3.4 copy-start.22
  132.0 2.0 copy-start.28
  134.1 2.1 copy-start.33
  136.1 2.0 copy-start.35
  138.9 12.1 %copy-start.13 = (bf16[512,1,5,128]{0,3,2,1:T(8,128)(2,1)S(1)}, bf16[512,1,5,128]{0,3,2,1:T(8,128)(2,1)}, u32[]{:S(2)}) copy-start(bf16[512,1,5,128]{0,3,2,1:T(8,128)(2,1)} %copy-done.12) | copy-start | bytes 1966084
  138.9 11.8 %copy-start.15 = (bf16[512,1,5,128]{0,3,2,1:T(8,128)(2,1)S(1)}, bf16[512,1,5,128]{0,3,2,1:T(8,128)(2,1)}, u32[]{:S(2)}) copy-start(bf16[512,1,5,128]{0,3,2,1:T(8,128)(2,1)} %copy-done.14) | copy-start | bytes 1966084
  138.9 19.3 %copy-start.38 = (bf16[1024,5120]{1,0:T(8,128)(2,1)S(1)}, bf16[1024,5120]{1,0:T(8,128)(2,1)}, u32[]{:S(2)}) copy-start(bf16[1024,5120]{1,0:T(8,128)(2,1)} %all-gather.2.cloned.1.call-done) | copy-start | bytes 31457284
  150.7 1.6 copy-start.3
  152.3 1.0 copy-start.34
  152.8 1.2 copy-start.4
  152.8 1.2 copy-start.10
  153.3 1.4 copy-start.6
  154.4 1.3 copy-start.7
  155.1 1.3 copy-start.8
  156.4 1.2 copy-start.5
  157.0 1.3 copy-start.17
  158.4 10.1 %copy-start = (f32[512,1024]{1,0:T(8,128)S(1)}, f32[512,1024]{1,0:T(8,128)}, u32[]{:S(2)}) copy-start(f32[512,1024]{1,0:T(8,128)} %subtract_exponential_fusion.1) | copy-start | bytes 6291460
  168.5 1.6 copy-start.1
  170.1 1.6 copy-start.2
  175.7 1.3 copy-start.30
  176.6 1.2 copy-start.27
  177.0 1.3 copy-start.23
  177.8 0.9 copy-start.21
  177.8 1.3 copy-start.19
  178.8 0.9 copy-start.25
  180.6 0.9 copy-start.36
  188.5 293.7 %all-to-all-start = ((bf16[8,128,896]{1,2,0:T(8,128)(2,1)}), bf16[8,128,896]{1,2,0:T(8,128)(2,1)S(1)}, u32[]{:S(2)}, u32[]{:S(2)}) async-start(bf16[8,128,896]{1,2,0:T(8,128)(2,1)} %copy.63), calls=%async_computation | async-start | bytes 3670016 | tf_op jit(solution)/shard_map/all_to_all | solution.py:190
  (1 other events, 0.9 us)
Sparse Core Ops, SparseCore 0:
  9.7 80.6 all-gather.1
